TPU v7x, 32 devices: a whole 2x2x4 slice. The times are simulated.
32 devices in a mesh: dp: 4 (over x, core), pipe: 2 (over y), tensor: 4 (over z).
Axes of the slice: x: 2, y: 2, z: 4, core: 2. Of those that a mesh axis runs over, the one named last changes fastest.
Arguments:
- layer_input: bfloat16 [4, 2, 512, 8192], P('dp', 'pipe', None, 'tensor'), may hold values from -40 to 40
- output_grad: bfloat16 [4, 2, 512, 8192], P('dp', 'pipe', None, 'tensor'), may hold values from -6 to 6
- kv_grad: bfloat16 [4, 2, 512, 2048], P('dp', 'pipe', None, 'tensor'), may hold values from -6 to 6
- norm_gain: bfloat16 [2, 8192], P('pipe', 'tensor'), may hold values from 0.5 to 1.5
- kv_weight: bfloat16 [2, 8192, 2048], P('pipe', 'tensor'), may hold values from -0.0625 to 0.0625
Outputs:
- upstream_grad: bfloat16 [4, 2, 512, 8192], P('dp', 'pipe', None, 'tensor')
- kv_weight_grad: bfloat16 [2, 8192, 2048], P('pipe', 'tensor', 'dp')
- gain_grad: float32 [2, 8192], P('pipe', 'tensor')
All inputs are finite; a program needn't handle non-finite values.
Results may differ from a plain program's by a relative error of at most 0.009.
Values may be sent and summed in bfloat16 or wider, within the bound.
No kernel may reach another device: no remote copies, remote signals or barrier semaphores. Data moves between devices by JAX's collectives and lax.ppermute only.
A program may use at most 128 MiB of HBM per device.

v0:
```python
import jax
import jax.numpy as jnp
from jax import lax
from jax.sharding import PartitionSpec as P

D = 8192


def from_behind(block, axis, distance):
    devices = range(lax.axis_size(axis))
    route = [(i - distance, i) for i in devices if i - distance in devices]
    return lax.ppermute(block, axis, route)


def on_device(layer_input, output_grad, kv_grad, norm_gain, kv_weight):
    rows = layer_input[0, 0]
    grad_out = output_grad[0, 0]
    grad_kv = kv_grad[0, 0]
    gain_f = norm_gain[0].astype(jnp.float32)
    weight = kv_weight[0]
    values = rows.astype(jnp.float32)
    local_squares = jnp.sum(values * values, axis=1, keepdims=True)
    total_squares = lax.psum(local_squares, "tensor")
    rstd = lax.rsqrt(total_squares / D + 1e-05)
    normed = values * rstd
    hidden = (normed * gain_f).astype(jnp.bfloat16)
    piece = lax.all_gather(grad_kv, "tensor", axis=1, tiled=True)
    row_total = lax.dot_general(
        piece, weight, (((1,), (1,)), ((), ())), preferred_element_type=jnp.float32
    )
    term = lax.dot_general(
        hidden, piece, (((0,), (0,)), ((), ())), preferred_element_type=jnp.float32
    )
    weight_total = term
    wgrad = weight_total
    scaled = gain_f * row_total
    local_dot = jnp.sum(scaled * normed, axis=1, keepdims=True)
    mean_term = lax.psum(local_dot, "tensor") / D
    input_grad = (grad_out.astype(jnp.float32) + rstd * (scaled - normed * mean_term)).astype(
        jnp.bfloat16
    )
    upstream = from_behind(input_grad, "pipe", -1)
    gain_part = jnp.sum(row_total * normed, axis=0)
    gain_total = lax.psum(gain_part, "dp")
    weight_total = lax.psum_scatter(
        wgrad.astype(jnp.bfloat16), "dp", scatter_dimension=1, tiled=True
    )
    return (upstream[None, None], weight_total[None], gain_total[None])


def solution(mesh):
    in_specs = (
        P("dp", "pipe", None, "tensor"),
        P("dp", "pipe", None, "tensor"),
        P("dp", "pipe", None, "tensor"),
        P("pipe", "tensor"),
        P("pipe", "tensor", None),
    )
    out_specs = (P("dp", "pipe", None, "tensor"), P("pipe", "tensor", "dp"), P("pipe", "tensor"))
    return jax.shard_map(
        on_device, mesh=mesh, in_specs=in_specs, out_specs=out_specs, check_vma=False
    )
```

profile of v0, /device:TPU:0, one launch (start us, length us, event | category | flops | bytes accessed | tf_op | source)
XLA Modules:
  0.0 152.9 jit_solution(5806783644709270451)
XLA Ops:
  7.2 0.0 all-gather.3.cloned.1.call-start
  7.2 0.7 all-gather.3.cloned.1.call-update
  7.9 0.0 reduce-scatter.2.cloned.1.call-start
  7.9 0.7 mul.69
  8.7 2.1 %fusion.13 = f32[512]{0:T(512)S(1)} fusion(bf16[1,1,512,2048]{3,2,1,0:T(8,128)(2,1)} %param.5), kind=kLoop, calls=%fused_computation.16 | loop fusion | flops 3145216 | bytes 2099200 | tf_op jit(solution)/shard_map/reduce_sum | solution.py:22
  10.7 13.7 %psum.21 = f32[512,1]{0,1:T(1,128)S(1)} all-reduce(f32[512,1]{0,1:T(1,128)S(1)} %bitcast.37), channel_id=1, replica_groups=mesh['dp'=4,'pipe'=2,'tensor'=4] {'tensor'}, use_global_device_ids=true, to_apply=%region_1.0 | all-reduce | flops 512 | bytes 4096 | tf_op jit(solution)/shard_map/psum | solution.py:23
  24.4 33.9 %all-gather.3.cloned.1.call-done = bf16[1,1,512,2048]{3,2,1,0:T(8,128)(2,1)} async-done(((bf16[1,1,512,512]{3,2,1,0:T(8,128)(2,1)}), bf16[1,1,512,2048]{3,2,1,0:T(8,128)(2,1)}) %all-gather.3.cloned.1.call-update) | async-done | bytes 2097168 | tf_op jit(solution)/shard_map/all_gather | solution.py:27
  58.3 10.1 %convolution_convert_fusion = bf16[2048,2048]{1,0:T(8,128)(2,1)} fusion(bf16[1,1,512,2048]{3,2,1,0:T(8,128)(2,1)} %param.5, bf16[1,1,512,2048]{3,2,1,0:T(8,128)(2,1)} %all-gather.3.cloned.1.call-done, f32[2048]{0:T(1024)S(1)} %bitcast.34, f32[512]{0:T(512)S(1)} %bitcast.39), kind=kOutput, calls=%fused_computation.2 | convolution fusion | flops 4303355904 | bytes 12593152 | tf_op jit(solution)/shard_map/dot_general | solution.py:31
  68.4 0.0 copy-start
  68.4 0.0 reduce-scatter.2.cloned.1.call-update
  68.4 1.6 %copy-done = bf16[1,1,512,2048]{3,2,1,0:T(8,128)(2,1)S(1)} copy-done((bf16[1,1,512,2048]{3,2,1,0:T(8,128)(2,1)S(1)}, bf16[1,1,512,2048]{3,2,1,0:T(8,128)(2,1)}, u32[]{:S(2)}) %copy-start) | copy-done | bytes 2097176
  70.0 11.8 %fusion.12 = (f32[2048]{0:T(1024)S(1)}, f32[512]{0:T(512)S(1)}, f32[512,2048]{1,0:T(8,128)}) fusion(bf16[1,1,512,2048]{3,2,1,0:T(8,128)(2,1)S(1)} %copy-done, f32[512]{0:T(512)S(1)} %bitcast.40, f32[2048]{0:T(1024)S(1)} %bitcast.35, bf16[1,2048,2048]{2,1,0:T(8,128)(2,1)} %param.9, bf16[1,1,512,2048]{3,2,1,0:T(8,128)(2,1)} %all-gather.3.cloned.1.call-done), kind=kOutput, calls=%fused_computation.15 | convolution fusion | flops 4302304768 | bytes 16797696 | tf_op jit(solution)/shard_map/dot_general | solution.py:28
  81.8 9.0 %psum.22 = f32[512,1]{0,1:T(1,128)S(1)} all-reduce(f32[512,1]{0,1:T(1,128)S(1)} %bitcast.43), channel_id=1, replica_groups=mesh['dp'=4,'pipe'=2,'tensor'=4] {'tensor'}, use_global_device_ids=true, to_apply=%region_3.0 | all-reduce | flops 512 | bytes 4096 | tf_op jit(solution)/shard_map/psum | solution.py:38
  90.8 5.7 %fusion.10 = bf16[512,2048]{1,0:T(8,128)(2,1)} fusion(f32[512,2048]{1,0:T(8,128)} %get-tuple-element.5, bf16[1,1,512,2048]{3,2,1,0:T(8,128)(2,1)} %param.6, bf16[1,1,512,2048]{3,2,1,0:T(8,128)(2,1)S(1)} %copy-done, f32[512]{0:T(512)S(1)} %bitcast.42, f32[2048]{0:T(1024)S(1)} %bitcast.36, f32[512]{0:T(512)S(1)} %bitcast.41), kind=kLoop, calls=%fused_computation.13 | loop fusion | flops 9437184 | bytes 10498048 | tf_op jit(solution)/shard_map/convert_element_type | solution.py:39
  96.5 1.3 collective-permute-start
  97.8 7.0 %psum.23 = f32[1,2048]{1,0:T(1,128)} all-reduce(f32[1,2048]{1,0:T(1,128)S(1)} %bitcast.38), channel_id=1, replica_groups=mesh['dp'=4,'pipe'=2,'tensor'=4] {'dp'}, use_global_device_ids=true, to_apply=%region_6.0 | all-reduce | flops 2048 | bytes 16384 | tf_op jit(solution)/shard_map/psum | solution.py:44
  104.8 39.9 %collective-permute-done = bf16[512,2048]{1,0:T(8,128)(2,1)S(1)} collective-permute-done((bf16[512,2048]{1,0:T(8,128)(2,1)}, bf16[512,2048]{1,0:T(8,128)(2,1)S(1)}, u32[]{:S(2)}, u32[]{:S(2)}) %collective-permute-start) | collective-permute-done | bytes 2097184 | tf_op jit(solution)/shard_map/ppermute | solution.py:12
  144.7 0.0 reduce-scatter.2.cloned.1.call-done
  144.7 1.3 copy.9
  (2 shorter events, 0.0 us)
Async XLA Ops:
  7.2 51.1 %all-gather.3.cloned.1.call-start = ((), (), s32[]{:S(2)}) async-start(), calls=%async_computation.2 | async-start | bytes 2621440 | tf_op jit(solution)/shard_map/all_gather | solution.py:27
  7.9 136.8 %reduce-scatter.2.cloned.1.call-start = ((), (), s32[]{:S(2)}) async-start(), calls=%async_computation.1 | async-start | bytes 10485760 | tf_op jit(solution)/shard_map/reduce_scatter | solution.py:45
  68.4 1.6 %copy-start = (bf16[1,1,512,2048]{3,2,1,0:T(8,128)(2,1)S(1)}, bf16[1,1,512,2048]{3,2,1,0:T(8,128)(2,1)}, u32[]{:S(2)}) copy-start(bf16[1,1,512,2048]{3,2,1,0:T(8,128)(2,1)} %param.5) | copy-start | bytes 6291460
  96.5 48.2 %collective-permute-start = (bf16[512,2048]{1,0:T(8,128)(2,1)}, bf16[512,2048]{1,0:T(8,128)(2,1)S(1)}, u32[]{:S(2)}, u32[]{:S(2)}) collective-permute-start(bf16[512,2048]{1,0:T(8,128)(2,1)} %fusion.10), channel_id=1, source_target_pairs={{4,0},{5,1},{6,2},{7,3},{12,8},{13,9},{14,10},{15,11},{20,16},{21,... | collective-permute-start | bytes 6291464 | tf_op jit(solution)/shard_map/ppermute | solution.py:12
Sparse Core Ops, SparseCore 0:
  9.6 48.6 all-gather.2
  68.5 70.6 reduce-scatter.1
where the time goes:
time: 153 us
  waiting for transfers between devices  74.5 us (49%)
  blocking collectives  29.6 us (19%)
  matrix products  21.9 us (14%)
  between operations  14.1 us (9%)
  other arithmetic  8.53 us (6%)
  local copies, waits for them, and re-layouts  2.89 us (2%)
    ppermute x1, waiting for transfers between devices, from_behind(): return lax.ppermute(block, axis, route)  39.9 us
    all_gather x1, waiting for transfers between devices, on_device(): piece = lax.all_gather(grad_kv, 'tensor', axis=1, tiled=True)  33.9 us
    psum x1, blocking collectives, on_device(): total_squares = lax.psum(local_squares, 'tensor')  13.7 us
    dot_general x1, matrix products, on_device(): lax.dot_general(piece, weight, (((1,), (1,)), ((), ())), preferred_elemen...  11.8 us
    dot_general x1, matrix products, on_device(): lax.dot_general(hidden, piece, (((0,), (0,)), ((), ())), preferred_elemen...  10.1 us
    psum x1, blocking collectives, on_device(): mean_term = lax.psum(local_dot, 'tensor') / D  8.96 us
    psum x1, blocking collectives, on_device(): gain_total = lax.psum(gain_part, 'dp')  7.03 us
    convert_element_type x1, other arithmetic, on_device(): (grad_out.astype(jnp.float32) + rstd * (scaled - normed * mean_term)).ast...  5.73 us
  transfers between devices with their start and end apart: 3, of which 2 were waited for; matrix products, arithmetic and copies ran while one was open for 13% of the time, Pallas kernels for 0%

commit v1 on v0

--- a/solution.py
+++ b/solution.py
@@ -24,7 +24,15 @@
     rstd = lax.rsqrt(total_squares / D + 1e-05)
     normed = values * rstd
     hidden = (normed * gain_f).astype(jnp.bfloat16)
-    piece = lax.all_gather(grad_kv, "tensor", axis=1, tiled=True)
+    ways, here, step = (lax.axis_size("tensor"), lax.axis_index("tensor"), grad_kv.shape[1])
+    line, have = (grad_kv, 1)
+    while have < ways:
+        line = jnp.concatenate(
+            [line, lax.ppermute(line, "tensor", [(d, (d - have) % ways) for d in range(ways)])],
+            axis=1,
+        )
+        have = 2 * have
+    piece = jnp.roll(line, here * step, axis=1)
     row_total = lax.dot_general(
         piece, weight, (((1,), (1,)), ((), ())), preferred_element_type=jnp.float32
     )

time: 153 us -> 170 us (1.11)
  blocking collectives: 29.6 us -> 45.3 us
  waiting for transfers between devices: 74.5 us -> 66.9 us
  starting transfers between devices: 1.36 us -> 7.78 us
  matrix products: 21.9 us -> 18.3 us
  local copies, waits for them, and re-layouts: 2.89 us -> 6.15 us
  other arithmetic: 8.53 us -> 11.3 us
    all_gather x1 -> x0, waiting for transfers between devices: 33.9 us -> none  [on_device(): piece = lax.all_gather(grad_kv, 'tensor', axis=1, tiled=True)]
    ppermute x0 -> x2, waiting for transfers between devices: none -> 29.9 us  [on_device(): lax.ppermute(line, 'tensor', [(d, (d - have) % ways) for d in range(ways)])]
    psum x1, blocking collectives: 13.7 us -> 25.2 us  [on_device(): total_squares = lax.psum(local_squares, 'tensor')]
    ppermute x0 -> x2, starting transfers between devices: none -> 6.47 us  [on_device(): lax.ppermute(line, 'tensor', [(d, (d - have) % ways) for d in range(ways)])]
    psum x1, blocking collectives: 8.96 us -> 13.1 us  [on_device(): mean_term = lax.psum(local_dot, 'tensor') / D]
    dot_general x1, matrix products: 10.1 us -> 7.1 us  [on_device(): lax.dot_general(hidden, piece, (((0,), (0,)), ((), ())), preferred_elemen...]
    ppermute x1, waiting for transfers between devices: 39.9 us -> 36.9 us  [from_behind(): return lax.ppermute(block, axis, route)]
    concatenate x0 -> x1, other arithmetic: none -> 2.16 us  [on_device(): jnp.concatenate([line, lax.ppermute(line, 'tensor', [(d, (d - have) % way...]
  transfers between devices with their start and end apart: 3 -> 4, of which waited for: 2 -> 3; matrix products, arithmetic and copies ran while one was open for 13% -> 12% of each run, Pallas kernels for 0% -> 0%
where the time goes in v1:
time: 170 us
  waiting for transfers between devices  66.9 us (39%)
  blocking collectives  45.3 us (27%)
  matrix products  18.3 us (11%)
  between operations  14.1 us (8%)
  other arithmetic  11.3 us (7%)
  starting transfers between devices  7.78 us (5%)
  local copies, waits for them, and re-layouts  6.15 us (4%)
    ppermute x1, waiting for transfers between devices, from_behind(): return lax.ppermute(block, axis, route)  36.9 us
    ppermute x2, waiting for transfers between devices, on_device(): lax.ppermute(line, 'tensor', [(d, (d - have) % ways) for d in range(ways)])  29.9 us
    psum x1, blocking collectives, on_device(): total_squares = lax.psum(local_squares, 'tensor')  25.2 us
    psum x1, blocking collectives, on_device(): mean_term = lax.psum(local_dot, 'tensor') / D  13.1 us
    dot_general x1, matrix products, on_device(): lax.dot_general(piece, weight, (((1,), (1,)), ((), ())), preferred_elemen...  11.2 us
    dot_general x1, matrix products, on_device(): lax.dot_general(hidden, piece, (((0,), (0,)), ((), ())), preferred_elemen...  7.1 us
    psum x1, blocking collectives, on_device(): gain_total = lax.psum(gain_part, 'dp')  7.03 us
    ppermute x2, starting transfers between devices, on_device(): lax.ppermute(line, 'tensor', [(d, (d - have) % ways) for d in range(ways)])  6.47 us
  transfers between devices with their start and end apart: 4, of which 3 were waited for; matrix products, arithmetic and copies ran while one was open for 12% of the time, Pallas kernels for 0%

profile of v1, /device:TPU:0, one launch (start us, length us, event | category | flops | bytes accessed | tf_op | source)
XLA Modules:
  0.0 169.8 jit_solution(7563995260880589670)
XLA Ops:
  7.2 0.0 copy-start.1
  7.2 0.0 reduce-scatter.2.cloned.1.call-start
  7.2 5.1 %collective-permute-start = (bf16[512,512]{1,0:T(8,128)(2,1)}, bf16[512,512]{1,0:T(8,128)(2,1)S(1)}, u32[]{:S(2)}, u32[]{:S(2)}) collective-permute-start(bf16[512,512]{1,0:T(8,128)(2,1)} %bitcast.29), channel_id=1, source_target_pairs={{0,3},{1,0},{2,1},{3,2},{4,7},{5,4},{6,5},{7,6},{8,11},{9,8},{10,9... | collective-permute-start | bytes 1572872 | tf_op jit(solution)/shard_map/ppermute | solution.py:31
  12.3 11.5 %collective-permute-done = bf16[512,512]{1,0:T(8,128)(2,1)S(1)} collective-permute-done((bf16[512,512]{1,0:T(8,128)(2,1)}, bf16[512,512]{1,0:T(8,128)(2,1)S(1)}, u32[]{:S(2)}, u32[]{:S(2)}) %collective-permute-start) | collective-permute-done | bytes 524320 | tf_op jit(solution)/shard_map/ppermute | solution.py:31
  23.8 2.2 %pad_maximum_fusion = bf16[512,1024]{1,0:T(8,128)(2,1)} fusion(bf16[512,512]{1,0:T(8,128)(2,1)S(1)} %collective-permute-done, bf16[512,512]{1,0:T(8,128)(2,1)} %bitcast.30), kind=kLoop, calls=%fused_computation.22 | loop fusion | flops 2097152 | bytes 2097152 | tf_op jit(solution)/shard_map/concatenate | solution.py:30
  26.0 1.4 collective-permute-start.1
  27.3 0.7 mul.73
  28.1 2.1 %fusion.13 = f32[512]{0:T(512)S(1)} fusion(bf16[1,1,512,2048]{3,2,1,0:T(8,128)(2,1)} %param.5), kind=kLoop, calls=%fused_computation.16 | loop fusion | flops 3145216 | bytes 2099200 | tf_op jit(solution)/shard_map/reduce_sum | solution.py:22
  30.1 25.2 %psum.21 = f32[512,1]{0,1:T(1,128)S(1)} all-reduce(f32[512,1]{0,1:T(1,128)S(1)} %bitcast.35), channel_id=1, replica_groups=mesh['dp'=4,'pipe'=2,'tensor'=4] {'tensor'}, use_global_device_ids=true, to_apply=%region_1.0 | all-reduce | flops 512 | bytes 4096 | tf_op jit(solution)/shard_map/psum | solution.py:23
  55.3 0.0 copy-done.1
  55.3 0.0 copy-start
  55.3 0.1 constant_dynamic-update-slice_fusion.5
  55.4 0.1 constant_dynamic-update-slice_fusion.4
  55.5 18.5 %collective-permute-done.1 = bf16[512,1024]{1,0:T(8,128)(2,1)} collective-permute-done((bf16[512,1024]{1,0:T(8,128)(2,1)}, bf16[512,1024]{1,0:T(8,128)(2,1)}, u32[]{:S(2)}, u32[]{:S(2)}) %collective-permute-start.1) | collective-permute-done | bytes 1048608 | tf_op jit(solution)/shard_map/ppermute | solution.py:31
  73.9 1.3 constant_dynamic-update-slice_fusion.3
  75.2 0.1 constant_dynamic-update-slice_fusion.2
  75.3 0.1 constant_dynamic-update-slice_fusion.1
  75.4 1.3 constant_dynamic-update-slice_fusion
  76.7 0.0 copy-start.2
  76.7 2.0 %copy-done.2 = bf16[512,4096]{1,0:T(8,128)(2,1)} copy-done((bf16[512,4096]{1,0:T(8,128)(2,1)}, bf16[512,4096]{1,0:T(8,128)(2,1)S(1)}, u32[]{:S(2)}) %copy-start.2) | copy-done | bytes 4194328
  78.7 0.0 copy-done
  78.7 7.1 %convolution_convert_fusion = bf16[2048,2048]{1,0:T(8,128)(2,1)} fusion(bf16[1,1,512,2048]{3,2,1,0:T(8,128)(2,1)S(1)} %copy-done, f32[2048]{0:T(1024)S(1)} %bitcast.32, f32[512]{0:T(512)S(1)} %bitcast.37, bf16[512,4096]{1,0:T(8,128)(2,1)S(1)} %constant_dynamic-update-slice_fusion, s32[]{:T(128)S(6)} %select_n.14), kind=kOutput, calls=%fused_computation.2 | convolution fusion | flops 4303355904 | bytes 12593156 | tf_op jit(solution)/shard_map/dot_general | solution.py:39
  85.8 0.0 reduce-scatter.2.cloned.1.call-update
  85.8 11.2 %fusion.12 = (f32[2048]{0:T(1024)S(1)}, f32[512]{0:T(512)S(1)}, f32[512,2048]{1,0:T(8,128)}) fusion(bf16[1,1,512,2048]{3,2,1,0:T(8,128)(2,1)S(1)} %copy-done, f32[512]{0:T(512)S(1)} %bitcast.38, f32[2048]{0:T(1024)S(1)} %bitcast.33, bf16[1,2048,2048]{2,1,0:T(8,128)(2,1)} %param.9, bf16[512,4096]{1,0:T(8,128)(2,1)} %copy-done.2, s32[]{:T(128)S(6)} %select_n.14), kind=kOutput, calls=%fused_computation.15 | convolution fusion | flops 4302304768 | bytes 16797700 | tf_op jit(solution)/shard_map/dot_general | solution.py:36
  97.0 13.1 %psum.22 = f32[512,1]{0,1:T(1,128)S(1)} all-reduce(f32[512,1]{0,1:T(1,128)S(1)} %bitcast.41), channel_id=1, replica_groups=mesh['dp'=4,'pipe'=2,'tensor'=4] {'tensor'}, use_global_device_ids=true, to_apply=%region_3.4 | all-reduce | flops 512 | bytes 4096 | tf_op jit(solution)/shard_map/psum | solution.py:46
  110.1 6.3 %fusion.10 = bf16[512,2048]{1,0:T(8,128)(2,1)} fusion(f32[512,2048]{1,0:T(8,128)} %get-tuple-element.5, bf16[1,1,512,2048]{3,2,1,0:T(8,128)(2,1)} %param.6, bf16[1,1,512,2048]{3,2,1,0:T(8,128)(2,1)S(1)} %copy-done, f32[512]{0:T(512)S(1)} %bitcast.40, f32[2048]{0:T(1024)S(1)} %bitcast.34, f32[512]{0:T(512)S(1)} %bitcast.39), kind=kLoop, calls=%fused_computation.13 | loop fusion | flops 9437184 | bytes 10498048 | tf_op jit(solution)/shard_map/convert_element_type | solution.py:47
  116.4 1.3 collective-permute-start.2
  117.7 7.0 %psum.23 = f32[1,2048]{1,0:T(1,128)} all-reduce(f32[1,2048]{1,0:T(1,128)S(1)} %bitcast.36), channel_id=1, replica_groups=mesh['dp'=4,'pipe'=2,'tensor'=4] {'dp'}, use_global_device_ids=true, to_apply=%region_6.7 | all-reduce | flops 2048 | bytes 16384 | tf_op jit(solution)/shard_map/psum | solution.py:52
  124.7 36.9 %collective-permute-done.2 = bf16[512,2048]{1,0:T(8,128)(2,1)S(1)} collective-permute-done((bf16[512,2048]{1,0:T(8,128)(2,1)}, bf16[512,2048]{1,0:T(8,128)(2,1)S(1)}, u32[]{:S(2)}, u32[]{:S(2)}) %collective-permute-start.2) | collective-permute-done | bytes 2097184 | tf_op jit(solution)/shard_map/ppermute | solution.py:12
  161.6 0.0 reduce-scatter.2.cloned.1.call-done
  161.6 1.3 copy.14
  (2 shorter events, 0.0 us)
Async XLA Ops:
  7.2 48.2 %copy-start.1 = (bf16[1,1,512,512]{3,2,1,0:T(8,128)(2,1)S(1)}, bf16[1,1,512,512]{3,2,1,0:T(8,128)(2,1)}, u32[]{:S(2)}) copy-start(bf16[1,1,512,512]{3,2,1,0:T(8,128)(2,1)} %param.7) | copy-start | bytes 1572868
  7.2 154.4 %reduce-scatter.2.cloned.1.call-start = ((), (), s32[]{:S(2)}) async-start(), calls=%async_computation.1 | async-start | bytes 10485760 | tf_op jit(solution)/shard_map/reduce_scatter | solution.py:53
  7.2 16.6 %collective-permute-start = (bf16[512,512]{1,0:T(8,128)(2,1)}, bf16[512,512]{1,0:T(8,128)(2,1)S(1)}, u32[]{:S(2)}, u32[]{:S(2)}) collective-permute-start(bf16[512,512]{1,0:T(8,128)(2,1)} %bitcast.29), channel_id=1, source_target_pairs={{0,3},{1,0},{2,1},{3,2},{4,7},{5,4},{6,5},{7,6},{8,11},{9,8},{10,9... | collective-permute-start | bytes 1572872 | tf_op jit(solution)/shard_map/ppermute | solution.py:31
  26.0 47.9 %collective-permute-start.1 = (bf16[512,1024]{1,0:T(8,128)(2,1)}, bf16[512,1024]{1,0:T(8,128)(2,1)}, u32[]{:S(2)}, u32[]{:S(2)}) collective-permute-start(bf16[512,1024]{1,0:T(8,128)(2,1)} %pad_maximum_fusion), channel_id=1, source_target_pairs={{0,2},{1,3},{2,0},{3,1},{4,6},{5,7},{6,4},{7,5},{8,10},{9,11},{10,... | collective-permute-start | bytes 3145736 | tf_op jit(solution)/shard_map/ppermute | solution.py:31
  55.3 23.3 %copy-start = (bf16[1,1,512,2048]{3,2,1,0:T(8,128)(2,1)S(1)}, bf16[1,1,512,2048]{3,2,1,0:T(8,128)(2,1)}, u32[]{:S(2)}) copy-start(bf16[1,1,512,2048]{3,2,1,0:T(8,128)(2,1)} %param.5) | copy-start | bytes 6291460
  76.7 2.0 %copy-start.2 = (bf16[512,4096]{1,0:T(8,128)(2,1)}, bf16[512,4096]{1,0:T(8,128)(2,1)S(1)}, u32[]{:S(2)}) copy-start(bf16[512,4096]{1,0:T(8,128)(2,1)S(1)} %constant_dynamic-update-slice_fusion) | copy-start | bytes 12582916
  116.4 45.2 %collective-permute-start.2 = (bf16[512,2048]{1,0:T(8,128)(2,1)}, bf16[512,2048]{1,0:T(8,128)(2,1)S(1)}, u32[]{:S(2)}, u32[]{:S(2)}) collective-permute-start(bf16[512,2048]{1,0:T(8,128)(2,1)} %fusion.10), channel_id=1, source_target_pairs={{4,0},{5,1},{6,2},{7,3},{12,8},{13,9},{14,10},{15,11},{20,16},{21,... | collective-permute-start | bytes 6291464 | tf_op jit(solution)/shard_map/ppermute | solution.py:12
Sparse Core Ops, SparseCore 0:
  85.9 74.2 reduce-scatter.1
